TPU v7x, 32 devices: a whole 2x2x4 slice. The times are simulated.
32 devices in a mesh: dp: 2 (over y), row: 4 (over x, core), col: 4 (over z).
Axes of the slice: x: 2, y: 2, z: 4, core: 2. Of those that a mesh axis runs over, the one named last changes fastest.
Arguments:
- patches: bfloat16 [2, 512, 1456], P('dp', 'col', 'row'), may hold values from -6 to 6
- queries: bfloat16 [2, 512, 6144], P('dp', 'col', 'row'), may hold values from -6 to 6
- attn_keys: bfloat16 [2, 512, 6144], P('dp', 'col', 'row'), may hold values from -6 to 6
- attn_values: bfloat16 [2, 512, 6144], P('dp', 'col', 'row'), may hold values from -6 to 6
- out_weight: bfloat16 [6144, 12288], P('row', 'col'), may hold values from -0.15625 to 0.15625
- output_grad: bfloat16 [2, 512, 12288], P('dp', 'row', 'col'), may hold values from -4 to 4
Outputs:
- query_grad: float32 [2, 512, 6144], P('dp', 'col', 'row')
- key_grad: float32 [2, 512, 6144], P('dp', 'col', 'row')
- value_grad: float32 [2, 512, 6144], P('dp', 'col', 'row')
- out_weight_grad: float32 [6144, 12288], P('row', 'col')
- embed_weight_grad: float32 [1456, 12288], P('row', 'col')
All inputs are finite; a program needn't handle non-finite values.
Results may differ from a plain program's by a relative error of at most 0.025.
Values may be sent and summed in bfloat16 or wider, within the bound.
No kernel may reach another device: no remote copies, remote signals or barrier semaphores. Data moves between devices by JAX's collectives and lax.ppermute only.
A program may use at most 128 MiB of HBM per device.

v0:
```python
import jax
import jax.numpy as jnp
from jax import lax
from jax.sharding import PartitionSpec as P

DH = 128


def contract_rows(left, right):
    return lax.dot_general(
        left, right, (((0,), (0,)), ((), ())), preferred_element_type=jnp.float32
    )


def body(patches, queries, attn_keys, attn_values, out_weight, output_grad):
    factor = DH ** (-0.5)
    local_rows = queries.shape[1]
    feature_width = queries.shape[2]
    head_count = feature_width // DH
    every_key, every_value, every_patch = (
        lax.all_gather(attn_keys, "col", axis=1, tiled=True),
        lax.all_gather(attn_values, "col", axis=1, tiled=True),
        lax.all_gather(patches, "col", axis=1, tiled=True),
    )
    local_query = queries[0].reshape(local_rows, head_count, DH)
    all_keys = every_key[0].reshape(-1, head_count, DH)
    all_values = every_value[0].reshape(-1, head_count, DH)
    scores = (
        jnp.einsum("qhd,khd->hqk", local_query, all_keys, preferred_element_type=jnp.float32)
        * factor
    )
    row_max = jnp.max(scores, axis=2, keepdims=True)
    log_total = row_max + jnp.log(jnp.sum(jnp.exp(scores - row_max), axis=2, keepdims=True))
    attn_probs = jnp.exp(scores - log_total).astype(jnp.bfloat16)
    attn_out = jnp.einsum(
        "hqk,khd->qhd", attn_probs, all_values, preferred_element_type=jnp.float32
    ).astype(jnp.bfloat16)
    out_local = attn_out.reshape(1, local_rows, feature_width)
    dense_grad = lax.all_gather(output_grad, "row", axis=1, tiled=True)[0]
    attn_grad = lax.psum_scatter(
        lax.dot_general(
            dense_grad, out_weight, (((1,), (1,)), ((), ())), preferred_element_type=jnp.float32
        ),
        "col",
        scatter_dimension=0,
        tiled=True,
    ).astype(jnp.bfloat16)
    grad_heads = attn_grad.reshape(local_rows, head_count, DH)
    prob_grad = jnp.einsum(
        "qhd,khd->hqk", grad_heads, all_values, preferred_element_type=jnp.float32
    )
    row_dot = jnp.transpose(
        jnp.sum(grad_heads.astype(jnp.float32) * attn_out.astype(jnp.float32), axis=2)
    )[:, :, None]
    score_grad = (attn_probs.astype(jnp.float32) * (prob_grad - row_dot)).astype(jnp.bfloat16)
    query_grad = (
        jnp.einsum("hqk,khd->qhd", score_grad, all_keys, preferred_element_type=jnp.float32)
        * factor
    )
    every_out = lax.all_gather(out_local, "col", axis=1, tiled=True)
    key_term = (
        jnp.einsum("hqk,qhd->khd", score_grad, local_query, preferred_element_type=jnp.float32)
        * factor
    )
    value_term = jnp.einsum(
        "hqk,qhd->khd", attn_probs, grad_heads, preferred_element_type=jnp.float32
    )
    key_sum, value_sum = (
        lax.psum_scatter(
            key_term.reshape(-1, feature_width).astype(jnp.bfloat16),
            "col",
            scatter_dimension=0,
            tiled=True,
        ).astype(jnp.float32),
        lax.psum_scatter(
            value_term.reshape(-1, feature_width).astype(jnp.bfloat16),
            "col",
            scatter_dimension=0,
            tiled=True,
        ).astype(jnp.float32),
    )
    out_part = contract_rows(every_out[0], dense_grad)
    embed_part = contract_rows(every_patch[0], dense_grad)
    out_weight_grad, embed_weight_grad = (
        lax.psum(out_part.astype(jnp.bfloat16), "dp").astype(jnp.float32),
        lax.psum(embed_part.astype(jnp.bfloat16), "dp").astype(jnp.float32),
    )
    return (
        query_grad.reshape(1, local_rows, feature_width),
        key_sum.reshape(1, local_rows, feature_width),
        value_sum.reshape(1, local_rows, feature_width),
        out_weight_grad,
        embed_weight_grad,
    )


def solution(mesh):
    placed = (
        P("dp", "col", "row"),
        P("dp", "col", "row"),
        P("dp", "col", "row"),
        P("dp", "col", "row"),
        P("row", "col"),
        P("dp", "row", "col"),
    )
    return jax.shard_map(
        body,
        mesh=mesh,
        in_specs=placed,
        out_specs=(
            P("dp", "col", "row"),
            P("dp", "col", "row"),
            P("dp", "col", "row"),
            P("row", "col"),
            P("row", "col"),
        ),
        check_vma=False,
    )
```

profile of v0, /device:TPU:0, one launch (start us, length us, event | category | flops | bytes accessed | tf_op | source)
XLA Modules:
  0.0 593.3 jit_solution(1535676170303104737)
XLA Ops:
  7.2 0.0 all-gather.7.cloned.1.call-start
  7.2 0.7 all-gather.7.cloned.1.call-update
  7.9 0.0 all-gather.5.cloned.1.call-start
  7.9 1.9 copy.22
  9.9 0.0 all-gather.5.cloned.1.call-update
  9.9 0.0 reduce-scatter.4.cloned.1.call-start
  9.9 30.9 %all-gather.7.cloned.1.call-done = bf16[1,512,3072]{2,1,0:T(8,128)(2,1)} async-done(((bf16[1,128,3072]{2,1,0:T(8,128)(2,1)}), bf16[1,512,3072]{2,1,0:T(8,128)(2,1)}) %all-gather.7.cloned.1.call-update) | async-done | bytes 3145744 | tf_op jit(solution)/shard_map/all_gather | solution.py:39
  40.8 10.6 %fusion.2 = f32[512,1536]{1,0:T(8,128)} fusion(bf16[1536,3072]{1,0:T(8,128)(2,1)} %param.10, bf16[1,512,3072]{2,1,0:T(8,128)(2,1)} %all-gather.7.cloned.1.call-done), kind=kOutput, calls=%fused_computation.4 | convolution fusion | flops 4831838208 | bytes 15728640 | tf_op jit(solution)/shard_map/dot_general | solution.py:41
  51.4 0.0 copy-start.3
  51.4 0.0 copy-start.4
  51.4 0.0 reduce-scatter.4.cloned.1.call-update
  51.4 0.0 all-gather.9.cloned.1.call-start
  51.5 0.9 copy-done.3
  52.4 0.9 copy.26
  53.3 0.0 all-gather.9.cloned.1.call-update
  53.4 0.0 all-gather.11.cloned.1.call-start
  53.4 0.0 copy-done.4
  53.4 0.2 copy.21
  53.6 0.0 copy-start.1
  53.7 27.0 %all-gather.5.cloned.1.call-done = bf16[1,512,1536]{1,2,0:T(8,128)(2,1)} async-done(((bf16[1,128,1536]{1,2,0:T(8,128)(2,1)}), bf16[1,512,1536]{1,2,0:T(8,128)(2,1)}) %all-gather.5.cloned.1.call-update) | async-done | bytes 1572880 | tf_op jit(solution)/shard_map/all_gather | solution.py:21
  80.7 2.1 multiply_reduce_fusion
  82.8 1.0 exponential_reduce_fusion
  83.8 0.0 copy-done.1
  83.8 0.5 exponential_convert_fusion
  84.4 57.7 %reduce-scatter.4.cloned.1.call-done = f32[128,1536]{1,0:T(8,128)} async-done(((f32[512,1536]{1,0:T(8,128)}), f32[128,1536]{1,0:T(8,128)}) %reduce-scatter.4.cloned.1.call-update) | async-done | bytes 786448 | tf_op jit(solution)/shard_map/reduce_scatter | solution.py:40
  142.1 1.2 convert_element_type.58
  143.3 0.2 copy.25
  143.5 38.4 %all-gather.9.cloned.1.call-done = bf16[1,512,1536]{1,2,0:T(8,128)(2,1)} async-done(((bf16[1,128,1536]{1,2,0:T(8,128)(2,1)}), bf16[1,512,1536]{1,2,0:T(8,128)(2,1)}) %all-gather.9.cloned.1.call-update) | async-done | bytes 1572880 | tf_op jit(solution)/shard_map/all_gather | solution.py:22
  181.9 2.7 multiply_reduce_fusion.1
  184.6 0.0 all-gather.11.cloned.1.call-update
  184.6 0.0 reduce-scatter.6.cloned.1.call-start
  184.7 2.0 multiply_convert_fusion.1
  186.7 2.7 multiply_convert_fusion
  189.4 2.7 copy.29
  192.1 0.0 reduce-scatter.6.cloned.1.call-update
  192.1 0.0 reduce-scatter.8.cloned.1.call-start
  192.1 1.7 convolution_convert_fusion.2
  193.8 0.0 copy-start.5
  193.8 2.6 copy.30
  196.5 0.0 reduce-scatter.8.cloned.1.call-update
  196.5 0.0 all-reduce.3.cloned.1.call-start
  196.6 0.0 copy-done.5
  196.6 20.1 %all_gather.19 = bf16[1,512,364]{1,2,0:T(8,128)(2,1)S(1)} all-gather(bf16[1,128,364]{1,2,0:T(8,128)(2,1)S(1)} %copy-done.5), channel_id=1, replica_groups=mesh['dp'=2,'row'=4,'col'=4] {'col'}, dimensions={1}, use_global_device_ids=true | all-gather | bytes 465920 | tf_op jit(solution)/shard_map/all_gather | solution.py:23
  216.7 4.6 convolution_convert_fusion.1
  221.3 5.5 all-gather.11.cloned.1.call-done
  226.8 9.3 %convolution_convert_fusion = bf16[1536,3072]{1,0:T(8,128)(2,1)} fusion(bf16[1,512,3072]{2,1,0:T(8,128)(2,1)} %all-gather.7.cloned.1.call-done, bf16[1,512,1536]{1,2,0:T(8,128)(2,1)} %all-gather.11.cloned.1.call-done), kind=kOutput, calls=%fused_computation | convolution fusion | flops 4836556800 | bytes 14155776 | tf_op jit(solution)/shard_map/dot_general | solution.py:10
  236.1 0.0 copy-start
  236.1 0.0 all-reduce.3.cloned.1.call-update
  236.1 1.4 copy-done
  237.5 1.5 convolution_multiply_fusion
  238.9 2.3 copy.31
  241.2 21.2 %reduce-scatter.6.cloned.1.call-done = bf16[128,1536]{1,0:T(8,128)(2,1)} async-done(((bf16[512,1536]{1,0:T(8,128)(2,1)}), bf16[128,1536]{1,0:T(8,128)(2,1)}) %reduce-scatter.6.cloned.1.call-update) | async-done | bytes 393232 | tf_op jit(solution)/shard_map/reduce_scatter | solution.py:69
  262.4 2.0 bitcast_convert_fusion.1
  264.4 34.6 %reduce-scatter.8.cloned.1.call-done = bf16[128,1536]{1,0:T(8,128)(2,1)} async-done(((bf16[512,1536]{1,0:T(8,128)(2,1)}), bf16[128,1536]{1,0:T(8,128)(2,1)}) %reduce-scatter.8.cloned.1.call-update) | async-done | bytes 393232 | tf_op jit(solution)/shard_map/reduce_scatter | solution.py:75
  299.0 2.0 bitcast_convert_fusion
  301.0 270.0 %all-reduce.3.cloned.1.call-done = (bf16[1536,3072]{1,0:T(8,128)(2,1)}, bf16[364,3072]{1,0:T(8,128)(2,1)}) async-done(((bf16[1536,3072]{1,0:T(8,128)(2,1)}, bf16[364,3072]{1,0:T(8,128)(2,1)}), (bf16[1536,3072]{1,0:T(8,128)(2,1)}, bf16[364,3072]{1,0:T(8,128)(2,1)})) %all-reduce.3.cloned.1.call-update) | async-done | bytes 11673616 | tf_op jit(solution)/shard_map/psum | solution.py:85
  571.0 0.0 copy-start.2
  571.0 12.9 %convert_element_type.71 = f32[1536,3072]{1,0:T(8,128)} convert(bf16[1536,3072]{1,0:T(8,128)(2,1)} %get-tuple-element.15) | non-fusion elementwise | flops 4718592 | bytes 28311552 | tf_op jit(solution)/shard_map/convert_element_type | solution.py:85
  583.8 0.0 copy-done.2
  583.8 2.7 convert_element_type.73
  (1 shorter events, 0.0 us)
Async XLA Ops:
  7.2 33.7 %all-gather.7.cloned.1.call-start = ((), (), s32[]{:S(2)}) async-start(), calls=%async_computation.4 | async-start | bytes 3932160 | tf_op jit(solution)/shard_map/all_gather | solution.py:39
  7.9 72.8 %all-gather.5.cloned.1.call-start = ((), (), s32[]{:S(2)}) async-start(), calls=%async_computation.3 | async-start | bytes 1966080 | tf_op jit(solution)/shard_map/all_gather | solution.py:21
  9.9 132.2 %reduce-scatter.4.cloned.1.call-start = ((), (), s32[]{:S(2)}) async-start(), calls=%async_computation.5 | async-start | bytes 3932160 | tf_op jit(solution)/shard_map/reduce_scatter | solution.py:40
  51.4 1.0 copy-start.3
  51.4 2.0 copy-start.4
  51.4 130.4 %all-gather.9.cloned.1.call-start = ((), (), s32[]{:S(2)}) async-start(), calls=%async_computation.6 | async-start | bytes 1966080 | tf_op jit(solution)/shard_map/all_gather | solution.py:22
  53.4 173.4 %all-gather.11.cloned.1.call-start = ((), (), s32[]{:S(2)}) async-start(), calls=%async_computation.9 | async-start | bytes 1966080 | tf_op jit(solution)/shard_map/all_gather | solution.py:60
  53.6 30.2 %copy-start.1 = (bf16[1,128,1536]{1,2,0:T(8,128)(2,1)}, bf16[1,128,1536]{1,2,0:T(8,128)(2,1)S(1)}, u32[]{:S(2)}) copy-start(bf16[1,128,1536]{1,2,0:T(8,128)(2,1)S(1)} %copy.21) | copy-start | bytes 1179652
  184.6 77.8 %reduce-scatter.6.cloned.1.call-start = ((), (), s32[]{:S(2)}) async-start(), calls=%async_computation.7 | async-start | bytes 1966080 | tf_op jit(solution)/shard_map/reduce_scatter | solution.py:69
  192.1 106.9 %reduce-scatter.8.cloned.1.call-start = ((), (), s32[]{:S(2)}) async-start(), calls=%async_computation.8 | async-start | bytes 1966080 | tf_op jit(solution)/shard_map/reduce_scatter | solution.py:75
  193.8 2.7 copy-start.5
  196.5 374.5 %all-reduce.3.cloned.1.call-start = ((), (), s32[]{:S(2)}) async-start(), calls=%async_computation.10 | async-start | bytes 23396352 | tf_op jit(solution)/shard_map/psum | solution.py:85
  236.1 1.4 copy-start
  571.0 12.9 %copy-start.2 = (bf16[364,3072]{1,0:T(8,128)(2,1)S(1)}, bf16[364,3072]{1,0:T(8,128)(2,1)}, u32[]{:S(2)}) copy-start(bf16[364,3072]{1,0:T(8,128)(2,1)} %get-tuple-element.16) | copy-start | bytes 6709252
Sparse Core Ops, SparseCore 0:
  9.6 31.2 all-gather.6
  43.0 37.7 all-gather.4
  83.6 58.4 reduce-scatter.3
  144.1 37.7 all-gather.8
  184.7 41.9 all-gather.10
  228.9 33.4 reduce-scatter.5
  264.7 34.2 reduce-scatter.7
  302.1 268.8 all-reduce.2
where the time goes:
time: 594 us; the launch traced here: 593 us
  waiting for transfers between devices  486 us (82%)
  matrix products  37.2 us (6%)
  other arithmetic  22.1 us (4%)
  blocking collectives  20.1 us (3%)
  between operations  14.2 us (2%)
  local copies, waits for them, and re-layouts  13.2 us (2%)
    psum x1, waiting for transfers between devices, body(): lax.psum(out_part.astype(jnp.bfloat16), 'dp').astype(jnp.float32)  270 us
    reduce_scatter x1, waiting for transfers between devices, body(): lax.psum_scatter(lax.dot_general(dense_grad, out_weight, (((1,), (1,)), (...  57.7 us
    all_gather x1, waiting for transfers between devices, body(): lax.all_gather(attn_values, 'col', axis=1, tiled=True)  38.4 us
    reduce_scatter x1, waiting for transfers between devices, body(): lax.psum_scatter(value_term.reshape(-1, feature_width).astype(jnp.bfloat1...  34.6 us
    all_gather x1, waiting for transfers between devices, body(): dense_grad = lax.all_gather(output_grad, 'row', axis=1, tiled=True)[0]  30.9 us
    all_gather x1, waiting for transfers between devices, body(): lax.all_gather(attn_keys, 'col', axis=1, tiled=True)  27 us
    reduce_scatter x1, waiting for transfers between devices, body(): lax.psum_scatter(key_term.reshape(-1, feature_width).astype(jnp.bfloat16)...  21.2 us
    all_gather x1, blocking collectives, body(): lax.all_gather(patches, 'col', axis=1, tiled=True)  20.1 us
  transfers between devices with their start and end apart: 8, of which 8 were waited for; matrix products, arithmetic and copies ran while one was open for 9% of the time, Pallas kernels for 0%

commit v1 on v0

--- a/solution.py
+++ b/solution.py
@@ -4,6 +4,23 @@
 from jax.sharding import PartitionSpec as P
 
 DH = 128
+
+
+def in_order(tiles, dim):
+    tiles = jnp.moveaxis(tiles, 0, dim)
+    dims = tiles.shape
+    return tiles.reshape(*dims[:dim], dims[dim] * dims[dim + 1], *dims[dim + 2 :])
+
+
+def ring_gather(x, axis, dim):
+    count = lax.axis_size(axis)
+    upward = [(i, (i + 1) % count) for i in range(count)]
+    blocks = [x]
+    while len(blocks) < count:
+        blocks.append(lax.ppermute(blocks[-1], axis, upward))
+    index = lax.axis_index(axis)
+    blocks = jnp.stack(blocks)[(index - jnp.arange(count)) % count]
+    return in_order(blocks, dim)
 
 
 def contract_rows(left, right):
@@ -19,7 +36,7 @@
     head_count = feature_width // DH
     every_key, every_value, every_patch = (
         lax.all_gather(attn_keys, "col", axis=1, tiled=True),
-        lax.all_gather(attn_values, "col", axis=1, tiled=True),
+        ring_gather(attn_values, "col", 1),
         lax.all_gather(patches, "col", axis=1, tiled=True),
     )
     local_query = queries[0].reshape(local_rows, head_count, DH)

time: 594 us -> 574 us (0.966)
  waiting for transfers between devices: 486 us -> 458 us
  local copies, waits for them, and re-layouts: 13.2 us -> 19.2 us
    ppermute x0 -> x3, waiting for transfers between devices: none -> 56.8 us  [ring_gather(): blocks.append(lax.ppermute(blocks[-1], axis, upward))]
    all_gather x1 -> x0, waiting for transfers between devices: 38.4 us -> none  [body(): lax.all_gather(attn_values, 'col', axis=1, tiled=True)]
    all_gather x1, waiting for transfers between devices: 27 us -> 0.02 us  [body(): lax.all_gather(attn_keys, 'col', axis=1, tiled=True)]
    reduce_scatter x1, waiting for transfers between devices: 57.7 us -> 39.5 us  [body(): lax.psum_scatter(lax.dot_general(dense_grad, out_weight, (((1,), (1,)), (...]
  transfers between devices with their start and end apart: 8 -> 10, of which waited for: 8 -> 9; matrix products, arithmetic and copies ran while one was open for 9% -> 10% of each run, Pallas kernels for 0% -> 0%
where the time goes in v1:
time: 574 us
  waiting for transfers between devices  458 us (80%)
  matrix products  35.4 us (6%)
  other arithmetic  23.1 us (4%)
  blocking collectives  20.2 us (4%)
  local copies, waits for them, and re-layouts  19.2 us (3%)
  between operations  14.3 us (2%)
    psum x1, waiting for transfers between devices, body(): lax.psum(out_part.astype(jnp.bfloat16), 'dp').astype(jnp.float32)  270 us
    ppermute x3, waiting for transfers between devices, ring_gather(): blocks.append(lax.ppermute(blocks[-1], axis, upward))  56.8 us
    reduce_scatter x1, waiting for transfers between devices, body(): lax.psum_scatter(lax.dot_general(dense_grad, out_weight, (((1,), (1,)), (...  39.5 us
    reduce_scatter x1, waiting for transfers between devices, body(): lax.psum_scatter(value_term.reshape(-1, feature_width).astype(jnp.bfloat1...  34.5 us
    all_gather x1, waiting for transfers between devices, body(): dense_grad = lax.all_gather(output_grad, 'row', axis=1, tiled=True)[0]  30.9 us
    reduce_scatter x1, waiting for transfers between devices, body(): lax.psum_scatter(key_term.reshape(-1, feature_width).astype(jnp.bfloat16)...  21.2 us
    all_gather x1, blocking collectives, body(): lax.all_gather(patches, 'col', axis=1, tiled=True)  20.2 us
    dot_general x2, matrix products, contract_rows(): lax.dot_general(left, right, (((0,), (0,)), ((), ())), preferred_element_...  13.9 us
  transfers between devices with their start and end apart: 10, of which 9 were waited for; matrix products, arithmetic and copies ran while one was open for 10% of the time, Pallas kernels for 0%

profile of v1, /device:TPU:0, one launch (start us, length us, event | category | flops | bytes accessed | tf_op | source)
XLA Modules:
  0.0 573.8 jit_solution(15533756566897115436)
XLA Ops:
  7.2 0.0 all-gather.6.cloned.1.call-start
  7.2 0.7 all-gather.6.cloned.1.call-update
  7.9 0.0 all-gather.4.cloned.1.call-start
  7.9 1.9 copy.23
  9.9 0.0 all-gather.4.cloned.1.call-update
  9.9 0.0 reduce-scatter.4.cloned.1.call-start
  9.9 30.9 %all-gather.6.cloned.1.call-done = bf16[1,512,3072]{2,1,0:T(8,128)(2,1)} async-done(((bf16[1,128,3072]{2,1,0:T(8,128)(2,1)}), bf16[1,512,3072]{2,1,0:T(8,128)(2,1)}) %all-gather.6.cloned.1.call-update) | async-done | bytes 3145744 | tf_op jit(solution)/shard_map/all_gather | solution.py:56
  40.8 10.6 %fusion.2 = f32[512,1536]{1,0:T(8,128)} fusion(bf16[1536,3072]{1,0:T(8,128)(2,1)} %param.10, bf16[1,512,3072]{2,1,0:T(8,128)(2,1)} %all-gather.6.cloned.1.call-done), kind=kOutput, calls=%fused_computation.5 | convolution fusion | flops 4831838208 | bytes 15728640 | tf_op jit(solution)/shard_map/dot_general | solution.py:58
  51.4 0.0 reduce-scatter.4.cloned.1.call-update
  51.4 0.0 all-gather.8.cloned.1.call-start
  51.5 0.9 copy-done.5
  52.4 1.5 collective-permute-start
  53.9 20.4 %collective-permute-done = bf16[1,128,1536]{2,1,0:T(8,128)(2,1)S(1)} collective-permute-done((bf16[1,128,1536]{2,1,0:T(8,128)(2,1)S(1)}, bf16[1,128,1536]{2,1,0:T(8,128)(2,1)S(1)}, u32[]{:S(2)}, u32[]{:S(2)}) %collective-permute-start) | collective-permute-done | bytes 393248 | tf_op jit(solution)/shard_map/ppermute | solution.py:20
  74.3 1.6 collective-permute-start.1
  76.0 21.4 %collective-permute-done.1 = bf16[1,128,1536]{2,1,0:T(8,128)(2,1)S(1)} collective-permute-done((bf16[1,128,1536]{2,1,0:T(8,128)(2,1)S(1)}, bf16[1,128,1536]{2,1,0:T(8,128)(2,1)S(1)}, u32[]{:S(2)}, u32[]{:S(2)}) %collective-permute-start.1) | collective-permute-done | bytes 393248 | tf_op jit(solution)/shard_map/ppermute | solution.py:20
  97.4 0.0 collective-permute-start.2
  97.4 0.0 copy-done.6
  97.4 0.2 copy.22
  97.6 0.0 copy-start.2
  97.6 14.9 %collective-permute-done.2 = bf16[1,128,1536]{2,1,0:T(8,128)(2,1)S(1)} collective-permute-done((bf16[1,128,1536]{2,1,0:T(8,128)(2,1)S(1)}, bf16[1,128,1536]{2,1,0:T(8,128)(2,1)S(1)}, u32[]{:S(2)}, u32[]{:S(2)}) %collective-permute-start.2) | collective-permute-done | bytes 393248 | tf_op jit(solution)/shard_map/ppermute | solution.py:20
  112.6 0.2 maximum_bitcast_fusion
  112.8 1.8 gather_fusion
  114.6 2.7 copy.27
  117.3 0.6 reshape_squeeze_reshape_transpose.3
  118.0 0.0 copy-start
  118.0 0.0 all-gather.4.cloned.1.call-done
  118.0 0.0 copy-done.2
  118.0 2.7 multiply_reduce_fusion
  120.7 1.0 exponential_reduce_fusion
  121.7 0.5 exponential_convert_fusion
  122.2 39.5 %reduce-scatter.4.cloned.1.call-done = f32[128,1536]{1,0:T(8,128)} async-done(((f32[512,1536]{1,0:T(8,128)}), f32[128,1536]{1,0:T(8,128)}) %reduce-scatter.4.cloned.1.call-update) | async-done | bytes 786448 | tf_op jit(solution)/shard_map/reduce_scatter | solution.py:57
  161.7 1.9 convert_element_type.58
  163.7 1.2 copy.26
  164.9 0.0 copy-done
  164.9 1.3 multiply_reduce_fusion.1
  166.2 0.0 all-gather.8.cloned.1.call-update
  166.2 0.0 reduce-scatter.6.cloned.1.call-start
  166.3 0.0 copy-start.3
  166.3 2.1 multiply_convert_fusion.1
  168.4 0.0 copy-done.3
  168.4 1.7 multiply_convert_fusion
  170.1 2.6 copy.30
  172.8 0.0 reduce-scatter.6.cloned.1.call-update
  172.8 0.0 reduce-scatter.8.cloned.1.call-start
  172.8 1.7 convolution_convert_fusion.2
  174.5 2.6 copy.31
  177.1 0.0 reduce-scatter.8.cloned.1.call-update
  177.2 0.0 all-reduce.3.cloned.1.call-start
  177.2 0.8 copy-done.7
  178.0 20.2 %all_gather.15 = bf16[1,512,364]{1,2,0:T(8,128)(2,1)S(1)} all-gather(bf16[1,128,364]{1,2,0:T(8,128)(2,1)S(1)} %copy-done.7), channel_id=1, replica_groups=mesh['dp'=2,'row'=4,'col'=4] {'col'}, dimensions={1}, use_global_device_ids=true | all-gather | bytes 465920 | tf_op jit(solution)/shard_map/all_gather | solution.py:40
  198.3 4.6 convolution_convert_fusion.1
  202.9 4.5 all-gather.8.cloned.1.call-done
  207.3 9.3 %convolution_convert_fusion = bf16[1536,3072]{1,0:T(8,128)(2,1)} fusion(bf16[1,512,3072]{2,1,0:T(8,128)(2,1)} %all-gather.6.cloned.1.call-done, bf16[1,512,1536]{1,2,0:T(8,128)(2,1)} %all-gather.8.cloned.1.call-done), kind=kOutput, calls=%fused_computation.1 | convolution fusion | flops 4836556800 | bytes 14155776 | tf_op jit(solution)/shard_map/dot_general | solution.py:27
  216.7 0.0 all-reduce.3.cloned.1.call-update
  216.7 1.4 copy-done.1
  218.1 1.5 convolution_multiply_fusion
  219.5 2.3 copy.32
  221.8 21.2 %reduce-scatter.6.cloned.1.call-done = bf16[128,1536]{1,0:T(8,128)(2,1)} async-done(((bf16[512,1536]{1,0:T(8,128)(2,1)}), bf16[128,1536]{1,0:T(8,128)(2,1)}) %reduce-scatter.6.cloned.1.call-update) | async-done | bytes 393232 | tf_op jit(solution)/shard_map/reduce_scatter | solution.py:86
  243.0 2.0 bitcast_convert_fusion.1
  245.0 34.5 %reduce-scatter.8.cloned.1.call-done = bf16[128,1536]{1,0:T(8,128)(2,1)} async-done(((bf16[512,1536]{1,0:T(8,128)(2,1)}), bf16[128,1536]{1,0:T(8,128)(2,1)}) %reduce-scatter.8.cloned.1.call-update) | async-done | bytes 393232 | tf_op jit(solution)/shard_map/reduce_scatter | solution.py:92
  279.5 2.0 bitcast_convert_fusion
  281.4 270.0 %all-reduce.3.cloned.1.call-done = (bf16[1536,3072]{1,0:T(8,128)(2,1)}, bf16[364,3072]{1,0:T(8,128)(2,1)}) async-done(((bf16[1536,3072]{1,0:T(8,128)(2,1)}, bf16[364,3072]{1,0:T(8,128)(2,1)}), (bf16[1536,3072]{1,0:T(8,128)(2,1)}, bf16[364,3072]{1,0:T(8,128)(2,1)})) %all-reduce.3.cloned.1.call-update) | async-done | bytes 11673616 | tf_op jit(solution)/shard_map/psum | solution.py:102
  551.4 12.9 %convert_element_type.71 = f32[1536,3072]{1,0:T(8,128)} convert(bf16[1536,3072]{1,0:T(8,128)(2,1)} %get-tuple-element.15) | non-fusion elementwise | flops 4718592 | bytes 28311552 | tf_op jit(solution)/shard_map/convert_element_type | solution.py:102
  564.3 2.7 convert_element_type.73
  (9 shorter events, 0.0 us)
Async XLA Ops:
  7.2 33.7 %all-gather.6.cloned.1.call-start = ((), (), s32[]{:S(2)}) async-start(), calls=%async_computation.4 | async-start | bytes 3932160 | tf_op jit(solution)/shard_map/all_gather | solution.py:56
  7.9 110.1 %all-gather.4.cloned.1.call-start = ((), (), s32[]{:S(2)}) async-start(), calls=%async_computation.3 | async-start | bytes 1966080 | tf_op jit(solution)/shard_map/all_gather | solution.py:38
  9.9 151.9 %reduce-scatter.4.cloned.1.call-start = ((), (), s32[]{:S(2)}) async-start(), calls=%async_computation.5 | async-start | bytes 3932160 | tf_op jit(solution)/shard_map/reduce_scatter | solution.py:57
  51.4 1.0 copy-start.5
  51.4 46.0 %copy-start.6 = (bf16[1,128,1536]{2,1,0:T(8,128)(2,1)S(1)}, bf16[1,128,1536]{2,1,0:T(8,128)(2,1)}, u32[]{:S(2)}) copy-start(bf16[1,128,1536]{2,1,0:T(8,128)(2,1)} %param.7) | copy-start | bytes 1179652
  51.4 155.9 %all-gather.8.cloned.1.call-start = ((), (), s32[]{:S(2)}) async-start(), calls=%async_computation.8 | async-start | bytes 1966080 | tf_op jit(solution)/shard_map/all_gather | solution.py:77
  52.4 21.9 %collective-permute-start = (bf16[1,128,1536]{2,1,0:T(8,128)(2,1)S(1)}, bf16[1,128,1536]{2,1,0:T(8,128)(2,1)S(1)}, u32[]{:S(2)}, u32[]{:S(2)}) collective-permute-start(bf16[1,128,1536]{2,1,0:T(8,128)(2,1)S(1)} %copy-done.5), channel_id=1, source_target_pairs={{0,1},{1,2},{2,3},{3,0},{4,5},{5,6},{6,7},{7,4},{8,9},{9,10},{10,1... | collective-permute-start | bytes 1179656 | tf_op jit(solution)/shard_map/ppermute | solution.py:20
  74.3 23.0 %collective-permute-start.1 = (bf16[1,128,1536]{2,1,0:T(8,128)(2,1)S(1)}, bf16[1,128,1536]{2,1,0:T(8,128)(2,1)S(1)}, u32[]{:S(2)}, u32[]{:S(2)}) collective-permute-start(bf16[1,128,1536]{2,1,0:T(8,128)(2,1)S(1)} %collective-permute-done), channel_id=1, source_target_pairs={{0,1},{1,2},{2,3},{3,0},{4,5},{5,6},{6,7},{7,4},{8,9},{9,10},{10,1... | collective-permute-start | bytes 1179656 | tf_op jit(solution)/shard_map/ppermute | solution.py:20
  97.4 15.2 %collective-permute-start.2 = (bf16[1,128,1536]{2,1,0:T(8,128)(2,1)S(1)}, bf16[1,128,1536]{2,1,0:T(8,128)(2,1)S(1)}, u32[]{:S(2)}, u32[]{:S(2)}) collective-permute-start(bf16[1,128,1536]{2,1,0:T(8,128)(2,1)S(1)} %collective-permute-done.1), channel_id=1, source_target_pairs={{0,1},{1,2},{2,3},{3,0},{4,5},{5,6},{6,7},{7,4},{8,9},{9,10},{10,1... | collective-permute-start | bytes 1179656 | tf_op jit(solution)/shard_map/ppermute | solution.py:20
  97.6 20.4 %copy-start.2 = (bf16[1,128,1536]{1,2,0:T(8,128)(2,1)}, bf16[1,128,1536]{1,2,0:T(8,128)(2,1)S(1)}, u32[]{:S(2)}) copy-start(bf16[1,128,1536]{1,2,0:T(8,128)(2,1)S(1)} %copy.22) | copy-start | bytes 1179652
  118.0 46.9 %copy-start = (bf16[512,12,128]{0,2,1:T(8,128)(2,1)}, bf16[512,12,128]{0,2,1:T(8,128)(2,1)S(1)}, u32[]{:S(2)}) copy-start(bf16[512,12,128]{0,2,1:T(8,128)(2,1)S(1)} %reshape_squeeze_reshape_transpose.3) | copy-start | bytes 4718596
  166.2 76.8 %reduce-scatter.6.cloned.1.call-start = ((), (), s32[]{:S(2)}) async-start(), calls=%async_computation.6 | async-start | bytes 1966080 | tf_op jit(solution)/shard_map/reduce_scatter | solution.py:86
  166.3 2.1 copy-start.3
  172.8 106.7 %reduce-scatter.8.cloned.1.call-start = ((), (), s32[]{:S(2)}) async-start(), calls=%async_computation.7 | async-start | bytes 1966080 | tf_op jit(solution)/shard_map/reduce_scatter | solution.py:92
  177.1 0.9 copy-start.7
  177.2 374.3 %all-reduce.3.cloned.1.call-start = ((), (), s32[]{:S(2)}) async-start(), calls=%async_computation.9 | async-start | bytes 23396352 | tf_op jit(solution)/shard_map/psum | solution.py:102
  216.7 1.4 copy-start.1
  551.4 12.9 %copy-start.4 = (bf16[364,3072]{1,0:T(8,128)(2,1)S(1)}, bf16[364,3072]{1,0:T(8,128)(2,1)}, u32[]{:S(2)}) copy-start(bf16[364,3072]{1,0:T(8,128)(2,1)} %get-tuple-element.16) | copy-start | bytes 6709252
Sparse Core Ops, SparseCore 0:
  9.6 31.2 all-gather.5
  43.0 52.9 all-gather.3
  98.8 62.8 reduce-scatter.3
  166.4 40.9 all-gather.7
  209.5 33.4 reduce-scatter.5
  245.2 34.2 reduce-scatter.7
  282.6 268.8 all-reduce.2
